TPU v7x, 256 devices: a whole 4x4x8 slice. The times are simulated.
256 devices in a mesh: lat: 8 (over y, z_lo), lon: 8 (over x, core), dp: 4 (over z_hi).
Axes of the slice: x: 4, y: 4, z: 8 (z_hi: 4, z_lo: 2; z = z_hi * 2 + z_lo), core: 2. Of those that a mesh axis runs over, the one named last changes fastest.
Arguments:
- state_grid: bfloat16 [4, 384, 768, 128], P('dp', ('lat', 'lon')), may hold values from -6 to 6
- cotangent: bfloat16 [4, 384, 768, 128], P('dp', ('lat', 'lon')), may hold values from -6 to 6
- legendre: bfloat16 [384, 384, 384], P(('lat', 'lon')), may hold values from -0.3125 to 0.3125
- wave_ids: int32 [384], replicated, may hold values from 0 to 383, each once
- weights: bfloat16 [384, 2, 4, 1024], P('lat'), may hold values from -0.75 to 0.75
Outputs:
- input_grad: bfloat16 [4, 384, 768, 128], P('dp', ('lat', 'lon'))
- weight_grad: float32 [384, 2, 4, 1024], P('lat')
Inputs may be any that keep to these rules, and one draw needn't show every extreme that they name: wave_ids[j] is the wavenumber of slot j; each of 0 to 383 stands in exactly one slot.
All inputs are finite; a program needn't handle non-finite values.
Results may differ from a plain program's by a relative error of at most 0.034.
Values may be sent and summed in bfloat16 or wider, within the bound.
No kernel may reach another device: no remote copies, remote signals or barrier semaphores. Data moves between devices by JAX's collectives and lax.ppermute only.
A program may use at most 128 MiB of HBM per device.

v0:
```python
import math
import jax
import jax.numpy as jnp
from jax import lax
from jax.sharding import PartitionSpec as P

NLON = 768
GROUPS = 4
GROUP_WIDTH = 32


def build_tables(wave_ids):
    columns = jnp.arange(NLON, dtype=jnp.int32)
    phase_int = wave_ids[:, None] * columns[None, :] % NLON
    angles = phase_int.astype(jnp.float32) * jnp.float32(2.0 * math.pi / NLON)
    factor = jnp.float32(1.0 / math.sqrt(NLON))
    paired = jnp.stack([jnp.cos(angles) * factor, -jnp.sin(angles) * factor], axis=1)
    forward_table = paired.reshape(2 * wave_ids.shape[0], NLON)
    doubling = jnp.where(wave_ids == 0, 1.0, 2.0).astype(jnp.float32)
    inverse_table = forward_table * jnp.repeat(doubling, 2)[:, None]
    return (forward_table.astype(jnp.bfloat16), inverse_table.astype(jnp.bfloat16))


def build_kernel(weights):
    degree_count = weights.shape[0]
    real_part = weights[:, 0].reshape(degree_count, GROUPS, GROUP_WIDTH, GROUP_WIDTH)
    imag_part = weights[:, 1].reshape(degree_count, GROUPS, GROUP_WIDTH, GROUP_WIDTH)
    upper_rows = jnp.stack([real_part, imag_part], axis=3)
    lower_rows = jnp.stack([-imag_part, real_part], axis=3)
    return jnp.stack([upper_rows, lower_rows], axis=2)


def gelu_slope(branch):
    normal_cdf = 0.5 * (1.0 + lax.erf(branch * (1.0 / math.sqrt(2.0))))
    density = jnp.exp(-0.5 * branch * branch) * (1.0 / math.sqrt(2.0 * math.pi))
    return normal_cdf + branch * density


def shards(state_grid, cotangent, legendre, wave_ids, weights):
    lat_count = lax.axis_size("lat")
    lon_count = lax.axis_size("lon")
    samples, rows_dev, lon_cells, channels = state_grid.shape
    slot_count, lat_cells, degree_count = legendre.shape
    slot_reals = 2 * slot_count
    first_slot = (lax.axis_index("lat") * lon_count + lax.axis_index("lon")) * slot_count
    held_waves = lax.dynamic_slice_in_dim(wave_ids, first_slot, slot_count)
    degree_ids = jnp.arange(degree_count, dtype=jnp.int32)
    masked = jnp.where(
        degree_ids[None, None, :] >= held_waves[:, None, None],
        legendre,
        jnp.zeros((), legendre.dtype),
    )
    slot_order = wave_ids.reshape(lat_count, lon_count, slot_count).transpose(1, 0, 2).reshape(-1)
    forward_table, inverse_table = build_tables(slot_order)
    kernel = build_kernel(weights)

    def analyze(source, twiddle):
        spectra = jnp.einsum(
            "srnc,kn->srkc", source, twiddle, preferred_element_type=jnp.float32
        ).astype(jnp.bfloat16)
        gathered = lax.all_to_all(
            lax.all_to_all(spectra, "lon", split_axis=2, concat_axis=1, tiled=True),
            "lat",
            split_axis=2,
            concat_axis=1,
            tiled=True,
        )
        blocks = gathered.reshape(samples, lat_cells, slot_count, 2 * channels)
        spectral = jnp.einsum("samc,mal->slmc", blocks, masked, preferred_element_type=jnp.float32)
        spectral = spectral.astype(jnp.bfloat16).reshape(
            samples, degree_count, slot_reals, channels
        )
        return lax.all_to_all(spectral, "lat", split_axis=1, concat_axis=2, tiled=True)

    def synthesize(spectral, twiddle):
        joined = lax.all_to_all(spectral, "lat", split_axis=2, concat_axis=1, tiled=True)
        blocks = joined.reshape(samples, degree_count, slot_count, 2 * channels)
        spectra = jnp.einsum(
            "slmc,mal->samc", blocks, masked, preferred_element_type=jnp.float32
        ).astype(jnp.bfloat16)
        spectra = spectra.reshape(samples, lat_cells, slot_reals, channels)
        pencil = lax.all_to_all(
            lax.all_to_all(spectra, "lat", split_axis=1, concat_axis=2, tiled=True),
            "lon",
            split_axis=1,
            concat_axis=2,
            tiled=True,
        )
        return jnp.einsum("srkc,kn->srnc", pencil, twiddle, preferred_element_type=jnp.float32)

    def split_groups(spectral):
        return spectral.reshape(samples, spectral.shape[1], -1, 2, GROUPS, GROUP_WIDTH)

    coef_fwd = analyze(state_grid, forward_table)
    coef_six = split_groups(coef_fwd)
    mixed_coef = jnp.einsum(
        "slmpgi,lgpiqo->slmqgo", coef_six, kernel, preferred_element_type=jnp.float32
    ).astype(jnp.bfloat16)
    branch = synthesize(mixed_coef.reshape(coef_fwd.shape), inverse_table)
    pulled = (cotangent.astype(jnp.float32) * gelu_slope(branch)).astype(jnp.bfloat16)
    back_coef = analyze(pulled, inverse_table)
    back_six = split_groups(back_coef)
    outer_sums = jnp.einsum(
        "slmpgi,slmqgo->lgpiqo", coef_six, back_six, preferred_element_type=jnp.float32
    )
    real_grad = outer_sums[:, :, 0, :, 0, :] + outer_sums[:, :, 1, :, 1, :]
    imag_grad = outer_sums[:, :, 0, :, 1, :] - outer_sums[:, :, 1, :, 0, :]
    local_grad = jnp.stack([real_grad, imag_grad], axis=1).reshape(weights.shape)
    weight_grad = lax.psum(local_grad.astype(jnp.bfloat16), ("lon", "dp")).astype(jnp.float32)
    demixed = jnp.einsum(
        "slmqgo,lgpiqo->slmpgi", back_six, kernel, preferred_element_type=jnp.float32
    ).astype(jnp.bfloat16)
    returned = synthesize(demixed.reshape(back_coef.shape), forward_table)
    input_grad = (cotangent.astype(jnp.float32) + returned).astype(jnp.bfloat16)
    return (input_grad, weight_grad)


def solution(mesh):
    return jax.shard_map(
        shards,
        mesh=mesh,
        in_specs=(
            P("dp", ("lat", "lon"), None, None),
            P("dp", ("lat", "lon"), None, None),
            P(("lat", "lon"), None, None),
            P(),
            P("lat", None, None, None),
        ),
        out_specs=(P("dp", ("lat", "lon"), None, None), P("lat", None, None, None)),
        check_vma=False,
    )
```

profile of v0, /device:TPU:8, one launch (start us, length us, event | category | flops | bytes accessed | tf_op | source)
XLA Modules:
  0.0 725.3 jit_solution(13457028617643623277)
XLA Ops:
  8.2 4.9 cosine_multiply_fusion
  15.6 3.7 reshape.366
  22.5 25.9 %all_to_all.192 = bf16[1,6,768,128]{3,1,0,2:T(8,128)(2,1)S(1)} all-to-all(bf16[1,6,768,128]{3,1,0,2:T(8,128)(2,1)S(1)} %copy.223), channel_id=1, replica_groups=mesh['lat'=8,'lon'=8,'dp'=4] {'lon'}, dimensions={2} | all-to-all | bytes 2359296 | tf_op jit(solution)/shard_map/all_to_all | solution.py:62
  50.1 6.5 all-to-all-start.1
  57.4 13.8 %all-to-all-done.1 = bf16[1,48,96,128]{3,1,0,2:T(8,128)(2,1)S(1)} async-done(((bf16[1,48,96,128]{3,1,0,2:T(8,128)(2,1)}), bf16[1,48,96,128]{3,1,0,2:T(8,128)(2,1)S(1)}, u32[]{:S(2)}, u32[]{:S(2)}) %all-to-all-start.1) | async-done | bytes 1179680 | tf_op jit(solution)/shard_map/all_to_all | solution.py:61
  71.2 3.0 copy.280
  74.2 4.4 reshape.378
  78.7 3.4 convolution_convert_fusion.1
  82.1 2.9 copy.229
  85.0 6.4 all-to-all-start.2
  100.2 3.0 pad_maximum_fusion
  103.2 12.7 %copy.232 = bf16[48,4,2,32,2,32]{3,5,2,4,1,0:T(8,128)(2,1)} copy(bf16[48,4,2,32,2,32]{0,5,4,3,1,2:T(8,128)(2,1)} %pad_maximum_fusion) | data formatting | bytes 3145728 | tf_op jit(solution)/shard_map/stack | solution.py:30
  120.3 8.3 %copy.270 = bf16[48,48,2,4,32,1]{1,4,2,5,3,0:T(8,128)(2,1)} copy(bf16[48,48,2,4,32,1]{0,4,3,2,1,5:T(8,128)(2,1)} %bitcast.179) | data formatting | bytes 2359296 | tf_op jit(solution)/shard_map/reshape.8
  128.5 6.7 fusion
  135.3 8.3 %copy.234 = bf16[1,48,48,2,4,32]{1,5,4,3,2,0:T(8,128)(2,1)} copy(bf16[1,48,48,2,4,32]{2,5,3,4,1,0:T(8,128)(2,1)} %fusion) | data formatting | bytes 2359296 | tf_op jit(solution)/shard_map/convert_element_type | solution.py:98
  143.5 3.2 copy.235
  146.7 19.4 %all_to_all.193 = bf16[1,48,96,128]{3,1,0,2:T(8,128)(2,1)} all-to-all(bf16[1,48,96,128]{3,1,0,2:T(8,128)(2,1)S(1)} %copy.235), channel_id=1, replica_groups=mesh['lat'=8,'lon'=8,'dp'=4] {'lat'}, dimensions={2} | all-to-all | bytes 2359296 | tf_op jit(solution)/shard_map/all_to_all | solution.py:76
  166.2 4.2 copy.283
  170.4 4.4 reshape.379
  174.8 3.5 convolution_convert_fusion.3
  178.3 2.9 copy.238
  181.2 21.5 %all_to_all.194 = bf16[1,384,12,128]{3,2,0,1:T(8,128)(2,1)S(1)} all-to-all(bf16[1,384,12,128]{3,2,0,1:T(8,128)(2,1)} %copy.238), channel_id=1, replica_groups=mesh['lat'=8,'lon'=8,'dp'=4] {'lat'}, dimensions={1} | all-to-all | bytes 2359296 | tf_op jit(solution)/shard_map/all_to_all | solution.py:83
  204.4 4.3 all-to-all-start.5
  211.1 14.9 %all-to-all-done.5 = bf16[1,48,96,128]{3,2,0,1:T(8,128)(2,1)} async-done(((bf16[1,48,96,128]{3,2,0,1:T(8,128)(2,1)}), bf16[1,48,96,128]{3,2,0,1:T(8,128)(2,1)}, u32[]{:S(2)}, u32[]{:S(2)}) %all-to-all-start.5) | async-done | bytes 1179680 | tf_op jit(solution)/shard_map/all_to_all | solution.py:82
  227.4 4.8 fusion.15
  234.4 24.2 %all_to_all.195 = bf16[1,6,768,128]{3,1,0,2:T(8,128)(2,1)S(1)} all-to-all(bf16[1,6,768,128]{3,1,0,2:T(8,128)(2,1)S(1)} %copy.244), channel_id=1, replica_groups=mesh['lat'=8,'lon'=8,'dp'=4] {'lon'}, dimensions={2} | all-to-all | bytes 2359296 | tf_op jit(solution)/shard_map/all_to_all | solution.py:62
  259.3 20.1 %all_to_all.196 = bf16[1,48,96,128]{3,1,0,2:T(8,128)(2,1)S(1)} all-to-all(bf16[1,48,96,128]{3,1,0,2:T(8,128)(2,1)S(1)} %copy.247), channel_id=1, replica_groups=mesh['lat'=8,'lon'=8,'dp'=4] {'lat'}, dimensions={2} | all-to-all | bytes 2359296 | tf_op jit(solution)/shard_map/all_to_all | solution.py:61
  279.4 3.0 copy.284
  282.4 4.4 reshape.380
  291.1 5.1 all-to-all-start.8
  296.3 11.6 %copy.253 = bf16[48,4,2,32,2,32]{5,3,4,2,1,0:T(8,128)(2,1)} copy(bf16[48,4,2,32,2,32]{0,5,4,3,1,2:T(8,128)(2,1)} %pad_maximum_fusion) | data formatting | bytes 3145728 | tf_op jit(solution)/shard_map/stack | solution.py:30
  307.8 6.3 all-to-all-done.8
  314.5 2.7 copy.252
  317.2 8.3 %copy.273 = bf16[48,48,2,4,32,1]{1,4,2,5,3,0:T(8,128)(2,1)} copy(bf16[48,48,2,4,32,1]{0,4,3,2,1,5:T(8,128)(2,1)} %bitcast.182) | data formatting | bytes 2359296 | tf_op jit(solution)/shard_map/reshape.39
  325.5 6.8 fusion.1
  332.3 8.3 %copy.255 = bf16[1,48,48,2,4,32]{1,5,4,3,2,0:T(8,128)(2,1)} copy(bf16[1,48,48,2,4,32]{2,5,3,4,1,0:T(8,128)(2,1)} %fusion.1) | data formatting | bytes 2359296 | tf_op jit(solution)/shard_map/convert_element_type | solution.py:112
  340.6 3.2 copy.256
  343.8 19.7 %all_to_all.197 = bf16[1,48,96,128]{3,1,0,2:T(8,128)(2,1)S(1)} all-to-all(bf16[1,48,96,128]{3,1,0,2:T(8,128)(2,1)S(1)} %copy.256), channel_id=1, replica_groups=mesh['lat'=8,'lon'=8,'dp'=4] {'lat'}, dimensions={2} | all-to-all | bytes 2359296 | tf_op jit(solution)/shard_map/all_to_all | solution.py:76
  363.5 3.0 copy.287
  366.4 4.4 reshape.381
  375.3 5.3 all-to-all-start.10
  380.6 8.3 %copy.276 = bf16[48,48,2,4,32,1]{1,4,5,2,3,0:T(8,128)(2,1)} copy(bf16[48,48,2,4,32,1]{0,4,3,2,1,5:T(8,128)(2,1)} %bitcast.180) | data formatting | bytes 2359296 | tf_op jit(solution)/shard_map/reshape.8
  388.9 12.5 %fusion.41 = f32[48,4,2,32,2,32]{5,3,4,2,1,0:T(8,128)} fusion(bf16[48,48,2,4,32,1]{1,4,5,2,3,0:T(8,128)(2,1)} %copy.276, bf16[48,48,2,4,32,1]{1,4,2,5,3,0:T(8,128)(2,1)} %copy.273), kind=kOutput, calls=%fused_computation.66 | convolution fusion | flops 75497472 | bytes 5505024 | tf_op jit(solution)/shard_map/slmpgi,slmqgo->lgpiqo/dot_general | solution.py:103
  403.1 4.3 all-to-all-start.11
  407.4 7.5 %fusion.3 = (bf16[48,4,1,32,1,32]{5,3,4,2,1,0:T(8,128)(2,1)}, bf16[48,4,1,32,1,32]{5,3,4,2,1,0:T(8,128)(2,1)S(1)}) fusion(f32[48,4,2,32,2,32]{5,3,4,2,1,0:T(8,128)} %fusion.41), kind=kLoop, calls=%fused_computation.9 | loop fusion | flops 786432 | bytes 3932160 | tf_op jit(solution)/shard_map/convert.3
  415.0 2.9 reshape.382
  421.6 290.0 %all-reduce.2.cloned.1.call-done = bf16[48,2,4,1024]{3,0,2,1:T(8,128)(2,1)} async-done(((bf16[48,2,4,1024]{3,0,2,1:T(8,128)(2,1)}), bf16[48,2,4,1024]{3,0,2,1:T(8,128)(2,1)}) %all-reduce.2.cloned.1.call-update) | async-done | bytes 786448 | tf_op jit(solution)/shard_map/psum | solution.py:109
  711.6 2.9 copy.269
  (62 shorter events, 48.9 us)
Async XLA Ops:
  7.2 12.2 %copy-start = (bf16[1,6,768,128]{3,2,1,0:T(8,128)(2,1)S(1)}, bf16[1,6,768,128]{3,2,1,0:T(8,128)(2,1)}, u32[]{:S(2)}) copy-start(bf16[1,6,768,128]{3,2,1,0:T(8,128)(2,1)} %param.5) | copy-start | bytes 3538948
  50.1 21.1 %all-to-all-start.1 = ((bf16[1,48,96,128]{3,1,0,2:T(8,128)(2,1)}), bf16[1,48,96,128]{3,1,0,2:T(8,128)(2,1)S(1)}, u32[]{:S(2)}, u32[]{:S(2)}) async-start(bf16[1,48,96,128]{3,1,0,2:T(8,128)(2,1)} %copy.226), calls=%async_computation.1 | async-start | bytes 2359296 | tf_op jit(solution)/shard_map/all_to_all | solution.py:61
  85.0 6.4 copy-start.3
  85.0 30.9 %all-to-all-start.2 = ((bf16[1,384,12,128]{3,2,0,1:T(8,128)(2,1)}), bf16[1,384,12,128]{3,2,0,1:T(8,128)(2,1)}, u32[]{:S(2)}, u32[]{:S(2)}) async-start(bf16[1,384,12,128]{3,2,0,1:T(8,128)(2,1)} %copy.229), calls=%async_computation.2 | async-start | bytes 3145728 | tf_op jit(solution)/shard_map/all_to_all | solution.py:73
  204.4 21.6 %all-to-all-start.5 = ((bf16[1,48,96,128]{3,2,0,1:T(8,128)(2,1)}), bf16[1,48,96,128]{3,2,0,1:T(8,128)(2,1)}, u32[]{:S(2)}, u32[]{:S(2)}) async-start(bf16[1,48,96,128]{3,2,0,1:T(8,128)(2,1)} %copy.241), calls=%async_computation.5 | async-start | bytes 2359296 | tf_op jit(solution)/shard_map/all_to_all | solution.py:82
  291.1 23.0 %all-to-all-start.8 = ((bf16[1,384,12,128]{3,2,0,1:T(8,128)(2,1)}), bf16[1,384,12,128]{3,2,0,1:T(8,128)(2,1)S(1)}, u32[]{:S(2)}, u32[]{:S(2)}) async-start(bf16[1,384,12,128]{3,2,0,1:T(8,128)(2,1)} %copy.250), calls=%async_computation.8 | async-start | bytes 3145728 | tf_op jit(solution)/shard_map/all_to_all | solution.py:73
  375.3 26.1 %all-to-all-start.10 = ((bf16[1,384,12,128]{3,2,0,1:T(8,128)(2,1)}), bf16[1,384,12,128]{3,2,0,1:T(8,128)(2,1)S(1)}, u32[]{:S(2)}, u32[]{:S(2)}) async-start(bf16[1,384,12,128]{3,2,0,1:T(8,128)(2,1)} %copy.259), calls=%async_computation.10 | async-start | bytes 3145728 | tf_op jit(solution)/shard_map/all_to_all | solution.py:83
  403.1 311.3 %all-to-all-start.11 = ((bf16[1,48,96,128]{3,2,0,1:T(8,128)(2,1)}), bf16[1,48,96,128]{3,2,0,1:T(8,128)(2,1)}, u32[]{:S(2)}, u32[]{:S(2)}) async-start(bf16[1,48,96,128]{3,2,0,1:T(8,128)(2,1)} %copy.262), calls=%async_computation.11 | async-start | bytes 2359296 | tf_op jit(solution)/shard_map/all_to_all | solution.py:82
  407.4 304.2 %all-reduce.2.cloned.1.call-start = ((), (), s32[]{:S(2)}) async-start(), calls=%async_computation.12 | async-start | bytes 1572864 | tf_op jit(solution)/shard_map/psum | solution.py:109
  419.5 1.6 copy-start.2
  714.5 1.6 copy-start.4
  716.1 2.1 copy-start.1
Sparse Core Ops, SparseCore 0:
  420.8 290.7 all-reduce.1
where the time goes:
time: 735 us; the launch traced here: 725 us
  waiting for transfers between devices  325 us (44%)
  local copies, waits for them, and re-layouts  155 us (21%)
  blocking collectives  131 us (18%)
  matrix products  47 us (6%)
  starting transfers between devices  31.8 us (4%)
  other arithmetic  20.7 us (3%)
  between operations  14.6 us (2%)
    psum x1, waiting for transfers between devices, shards(): lax.psum(local_grad.astype(jnp.bfloat16), ('lon', 'dp')).astype(jnp.float32)  290 us
    another operation x11, local copies, waits for them, and re-layouts  55.7 us
    all_to_all x2, blocking collectives, analyze(): lax.all_to_all(spectra, 'lon', split_axis=2, concat_axis=1, tiled=True)  50.1 us
    all_to_all x2, blocking collectives, synthesize(): lax.all_to_all(spectral, 'lat', split_axis=2, concat_axis=1, tiled=True)  39.1 us
    another operation x2, local copies, waits for them, and re-layouts, build_kernel(): return jnp.stack([upper_rows, lower_rows], axis=2)  24.2 us
    all_to_all x1, blocking collectives, synthesize(): lax.all_to_all(spectra, 'lat', split_axis=1, concat_axis=2, tiled=True)  21.5 us
    all_to_all x1, blocking collectives, analyze(): lax.all_to_all(lax.all_to_all(spectra, 'lon', split_axis=2, concat_axis=1...  20.1 us
    all_to_all x2, waiting for transfers between devices, synthesize(): lax.all_to_all(lax.all_to_all(spectra, 'lat', split_axis=1, concat_axis=2...  14.9 us
  transfers between devices with their start and end apart: 7, of which 4 were waited for; matrix products, arithmetic and copies ran while one was open for 11% of the time, Pallas kernels for 0%

commit v1 on v0

--- a/solution.py
+++ b/solution.py
@@ -106,7 +106,9 @@
     real_grad = outer_sums[:, :, 0, :, 0, :] + outer_sums[:, :, 1, :, 1, :]
     imag_grad = outer_sums[:, :, 0, :, 1, :] - outer_sums[:, :, 1, :, 0, :]
     local_grad = jnp.stack([real_grad, imag_grad], axis=1).reshape(weights.shape)
-    weight_grad = lax.psum(local_grad.astype(jnp.bfloat16), ("lon", "dp")).astype(jnp.float32)
+    weight_grad = lax.psum(lax.psum(local_grad.astype(jnp.bfloat16), "lon"), "dp").astype(
+        jnp.float32
+    )
     demixed = jnp.einsum(
         "slmqgo,lgpiqo->slmpgi", back_six, kernel, preferred_element_type=jnp.float32
     ).astype(jnp.bfloat16)

time: 735 us -> 563 us (0.77)
  waiting for transfers between devices: 325 us -> 161 us
    psum x1 -> x2, waiting for transfers between devices: 290 us -> 126 us  [the longest x1 64.9 us: shards(): lax.psum(local_grad.astype(jnp.bfloat16), 'lon')]
  transfers between devices with their start and end apart: 7 -> 8, of which waited for: 4 -> 5; matrix products, arithmetic and copies ran while one was open for 11% -> 13% of each run, Pallas kernels for 0% -> 0%
where the time goes in v1:
time: 563 us; the launch traced here: 552 us
  waiting for transfers between devices  161 us (29%)
  local copies, waits for them, and re-layouts  156 us (28%)
  blocking collectives  131 us (23%)
  matrix products  42.4 us (8%)
  starting transfers between devices  31.2 us (6%)
  other arithmetic  16.4 us (3%)
  between operations  14.6 us (3%)
    psum x1, waiting for transfers between devices, shards(): lax.psum(local_grad.astype(jnp.bfloat16), 'lon')  64.9 us
    psum x1, waiting for transfers between devices, shards(): lax.psum(lax.psum(local_grad.astype(jnp.bfloat16), 'lon'), 'dp')  61.3 us
    another operation x11, local copies, waits for them, and re-layouts  55.6 us
    all_to_all x2, blocking collectives, analyze(): lax.all_to_all(spectra, 'lon', split_axis=2, concat_axis=1, tiled=True)  50.1 us
    all_to_all x2, blocking collectives, synthesize(): lax.all_to_all(spectral, 'lat', split_axis=2, concat_axis=1, tiled=True)  39.1 us
    another operation x2, local copies, waits for them, and re-layouts, build_kernel(): return jnp.stack([upper_rows, lower_rows], axis=2)  24.2 us
    all_to_all x1, blocking collectives, synthesize(): lax.all_to_all(spectra, 'lat', split_axis=1, concat_axis=2, tiled=True)  21.5 us
    all_to_all x1, blocking collectives, analyze(): lax.all_to_all(lax.all_to_all(spectra, 'lon', split_axis=2, concat_axis=1...  20.1 us
  transfers between devices with their start and end apart: 8, of which 5 were waited for; matrix products, arithmetic and copies ran while one was open for 13% of the time, Pallas kernels for 0%

profile of v1, /device:TPU:8, one launch (start us, length us, event | category | flops | bytes accessed | tf_op | source)
XLA Modules:
  0.0 552.5 jit_solution(8054474275673524559)
XLA Ops:
  8.2 4.9 cosine_multiply_fusion
  15.6 3.7 reshape.366
  22.5 25.9 %all_to_all.192 = bf16[1,6,768,128]{3,1,0,2:T(8,128)(2,1)S(1)} all-to-all(bf16[1,6,768,128]{3,1,0,2:T(8,128)(2,1)S(1)} %copy.223), channel_id=1, replica_groups=mesh['lat'=8,'lon'=8,'dp'=4] {'lon'}, dimensions={2} | all-to-all | bytes 2359296 | tf_op jit(solution)/shard_map/all_to_all | solution.py:62
  50.1 6.5 %all-to-all-start.1 = ((bf16[1,48,96,128]{3,1,0,2:T(8,128)(2,1)}), bf16[1,48,96,128]{3,1,0,2:T(8,128)(2,1)S(1)}, u32[]{:S(2)}, u32[]{:S(2)}) async-start(bf16[1,48,96,128]{3,1,0,2:T(8,128)(2,1)} %copy.226), calls=%async_computation.1 | async-start | bytes 2359296 | tf_op jit(solution)/shard_map/all_to_all | solution.py:61
  57.4 13.8 %all-to-all-done.1 = bf16[1,48,96,128]{3,1,0,2:T(8,128)(2,1)S(1)} async-done(((bf16[1,48,96,128]{3,1,0,2:T(8,128)(2,1)}), bf16[1,48,96,128]{3,1,0,2:T(8,128)(2,1)S(1)}, u32[]{:S(2)}, u32[]{:S(2)}) %all-to-all-start.1) | async-done | bytes 1179680 | tf_op jit(solution)/shard_map/all_to_all | solution.py:61
  71.2 3.0 copy.280
  74.2 4.4 reshape.378
  78.7 3.4 convolution_convert_fusion.1
  82.1 2.9 copy.229
  85.0 6.4 %all-to-all-start.2 = ((bf16[1,384,12,128]{3,2,0,1:T(8,128)(2,1)}), bf16[1,384,12,128]{3,2,0,1:T(8,128)(2,1)}, u32[]{:S(2)}, u32[]{:S(2)}) async-start(bf16[1,384,12,128]{3,2,0,1:T(8,128)(2,1)} %copy.229), calls=%async_computation.2 | async-start | bytes 3145728 | tf_op jit(solution)/shard_map/all_to_all | solution.py:73
  100.2 3.0 pad_maximum_fusion
  103.2 12.7 %copy.232 = bf16[48,4,2,32,2,32]{3,5,2,4,1,0:T(8,128)(2,1)} copy(bf16[48,4,2,32,2,32]{0,5,4,3,1,2:T(8,128)(2,1)} %pad_maximum_fusion) | data formatting | bytes 3145728 | tf_op jit(solution)/shard_map/stack | solution.py:30
  120.3 8.3 %copy.270 = bf16[48,48,2,4,32,1]{1,4,2,5,3,0:T(8,128)(2,1)} copy(bf16[48,48,2,4,32,1]{0,4,3,2,1,5:T(8,128)(2,1)} %bitcast.179) | data formatting | bytes 2359296 | tf_op jit(solution)/shard_map/reshape.8
  128.5 6.7 %fusion = bf16[1,48,48,2,4,32]{2,5,3,4,1,0:T(8,128)(2,1)} fusion(bf16[48,4,2,32,2,32]{3,5,2,4,1,0:T(8,128)(2,1)} %copy.232, bf16[48,48,2,4,32,1]{1,4,2,5,3,0:T(8,128)(2,1)} %copy.270), kind=kOutput, calls=%fused_computation.4 | convolution fusion | flops 76087296 | bytes 3932160 | tf_op jit(solution)/shard_map/slmpgi,lgpiqo->slmqgo/dot_general | solution.py:96
  135.3 8.3 %copy.234 = bf16[1,48,48,2,4,32]{1,5,4,3,2,0:T(8,128)(2,1)} copy(bf16[1,48,48,2,4,32]{2,5,3,4,1,0:T(8,128)(2,1)} %fusion) | data formatting | bytes 2359296 | tf_op jit(solution)/shard_map/convert_element_type | solution.py:98
  143.5 3.2 copy.235
  146.7 19.4 %all_to_all.193 = bf16[1,48,96,128]{3,1,0,2:T(8,128)(2,1)} all-to-all(bf16[1,48,96,128]{3,1,0,2:T(8,128)(2,1)S(1)} %copy.235), channel_id=1, replica_groups=mesh['lat'=8,'lon'=8,'dp'=4] {'lat'}, dimensions={2} | all-to-all | bytes 2359296 | tf_op jit(solution)/shard_map/all_to_all | solution.py:76
  166.2 4.2 copy.283
  170.4 4.4 reshape.379
  174.8 3.5 convolution_convert_fusion.3
  178.3 2.9 copy.238
  181.2 21.5 %all_to_all.194 = bf16[1,384,12,128]{3,2,0,1:T(8,128)(2,1)S(1)} all-to-all(bf16[1,384,12,128]{3,2,0,1:T(8,128)(2,1)} %copy.238), channel_id=1, replica_groups=mesh['lat'=8,'lon'=8,'dp'=4] {'lat'}, dimensions={1} | all-to-all | bytes 2359296 | tf_op jit(solution)/shard_map/all_to_all | solution.py:83
  204.4 4.3 all-to-all-start.5
  211.1 14.9 %all-to-all-done.5 = bf16[1,48,96,128]{3,2,0,1:T(8,128)(2,1)} async-done(((bf16[1,48,96,128]{3,2,0,1:T(8,128)(2,1)}), bf16[1,48,96,128]{3,2,0,1:T(8,128)(2,1)}, u32[]{:S(2)}, u32[]{:S(2)}) %all-to-all-start.5) | async-done | bytes 1179680 | tf_op jit(solution)/shard_map/all_to_all | solution.py:82
  227.4 4.8 fusion.15
  234.4 24.2 %all_to_all.195 = bf16[1,6,768,128]{3,1,0,2:T(8,128)(2,1)S(1)} all-to-all(bf16[1,6,768,128]{3,1,0,2:T(8,128)(2,1)S(1)} %copy.244), channel_id=1, replica_groups=mesh['lat'=8,'lon'=8,'dp'=4] {'lon'}, dimensions={2} | all-to-all | bytes 2359296 | tf_op jit(solution)/shard_map/all_to_all | solution.py:62
  259.3 20.1 %all_to_all.196 = bf16[1,48,96,128]{3,1,0,2:T(8,128)(2,1)S(1)} all-to-all(bf16[1,48,96,128]{3,1,0,2:T(8,128)(2,1)S(1)} %copy.247), channel_id=1, replica_groups=mesh['lat'=8,'lon'=8,'dp'=4] {'lat'}, dimensions={2} | all-to-all | bytes 2359296 | tf_op jit(solution)/shard_map/all_to_all | solution.py:61
  279.4 3.0 copy.284
  282.4 4.4 reshape.380
  291.1 5.1 all-to-all-start.8
  296.3 11.6 %copy.253 = bf16[48,4,2,32,2,32]{5,3,4,2,1,0:T(8,128)(2,1)} copy(bf16[48,4,2,32,2,32]{0,5,4,3,1,2:T(8,128)(2,1)} %pad_maximum_fusion) | data formatting | bytes 3145728 | tf_op jit(solution)/shard_map/stack | solution.py:30
  307.8 6.3 %all-to-all-done.8 = bf16[1,384,12,128]{3,2,0,1:T(8,128)(2,1)S(1)} async-done(((bf16[1,384,12,128]{3,2,0,1:T(8,128)(2,1)}), bf16[1,384,12,128]{3,2,0,1:T(8,128)(2,1)S(1)}, u32[]{:S(2)}, u32[]{:S(2)}) %all-to-all-start.8) | async-done | bytes 1179680 | tf_op jit(solution)/shard_map/all_to_all | solution.py:73
  317.2 8.2 %copy.273 = bf16[48,48,2,4,32,1]{1,4,2,5,3,0:T(8,128)(2,1)} copy(bf16[48,48,2,4,32,1]{0,4,3,2,1,5:T(8,128)(2,1)} %bitcast.182) | data formatting | bytes 2359296 | tf_op jit(solution)/shard_map/reshape.39
  325.5 6.7 %fusion.1 = bf16[1,48,48,2,4,32]{2,5,3,4,1,0:T(8,128)(2,1)} fusion(bf16[48,4,2,32,2,32]{5,3,4,2,1,0:T(8,128)(2,1)} %copy.253, bf16[48,48,2,4,32,1]{1,4,2,5,3,0:T(8,128)(2,1)} %copy.273), kind=kOutput, calls=%fused_computation.5 | convolution fusion | flops 76087296 | bytes 3932160 | tf_op jit(solution)/shard_map/slmqgo,lgpiqo->slmpgi/dot_general | solution.py:112
  332.2 8.3 %copy.255 = bf16[1,48,48,2,4,32]{1,5,4,3,2,0:T(8,128)(2,1)} copy(bf16[1,48,48,2,4,32]{2,5,3,4,1,0:T(8,128)(2,1)} %fusion.1) | data formatting | bytes 2359296 | tf_op jit(solution)/shard_map/convert_element_type | solution.py:114
  340.4 3.2 copy.256
  343.6 19.7 %all_to_all.197 = bf16[1,48,96,128]{3,1,0,2:T(8,128)(2,1)S(1)} all-to-all(bf16[1,48,96,128]{3,1,0,2:T(8,128)(2,1)S(1)} %copy.256), channel_id=1, replica_groups=mesh['lat'=8,'lon'=8,'dp'=4] {'lat'}, dimensions={2} | all-to-all | bytes 2359296 | tf_op jit(solution)/shard_map/all_to_all | solution.py:76
  363.3 3.0 copy.287
  366.3 4.4 reshape.381
  375.2 5.1 all-to-all-start.10
  380.5 8.3 %copy.276 = bf16[48,48,2,4,32,1]{1,4,5,2,3,0:T(8,128)(2,1)} copy(bf16[48,48,2,4,32,1]{0,4,3,2,1,5:T(8,128)(2,1)} %bitcast.180) | data formatting | bytes 2359296 | tf_op jit(solution)/shard_map/reshape.8
  388.7 8.0 %fusion.41 = f32[48,4,2,32,2,32]{5,3,4,2,1,0:T(8,128)S(1)} fusion(bf16[48,48,2,4,32,1]{1,4,5,2,3,0:T(8,128)(2,1)} %copy.276, bf16[48,48,2,4,32,1]{1,4,2,5,3,0:T(8,128)(2,1)} %copy.273), kind=kOutput, calls=%fused_computation.66 | convolution fusion | flops 75497472 | bytes 5505024 | tf_op jit(solution)/shard_map/slmpgi,slmqgo->lgpiqo/dot_general | solution.py:103
  396.7 3.2 fusion.3
  402.9 2.9 reshape.383
  408.7 3.7 all-to-all-start.11
  412.4 64.9 %all-reduce.3.cloned.1.call-done = bf16[48,2,4,1024]{3,0,2,1:T(8,128)(2,1)} async-done(((bf16[48,2,4,1024]{3,0,2,1:T(8,128)(2,1)}), bf16[48,2,4,1024]{3,0,2,1:T(8,128)(2,1)}) %all-reduce.3.cloned.1.call-update) | async-done | bytes 786448 | tf_op jit(solution)/shard_map/psum | solution.py:109
  477.9 61.3 %all-reduce.5.cloned.1.call-done = bf16[48,2,4,1024]{3,0,2,1:T(8,128)(2,1)} async-done(((bf16[48,2,4,1024]{3,0,2,1:T(8,128)(2,1)}), bf16[48,2,4,1024]{3,0,2,1:T(8,128)(2,1)}) %all-reduce.5.cloned.1.call-update) | async-done | bytes 786448 | tf_op jit(solution)/shard_map/psum | solution.py:109
  539.1 2.9 copy.269
  (65 shorter events, 52.4 us)
Async XLA Ops:
  7.2 12.2 %copy-start = (bf16[1,6,768,128]{3,2,1,0:T(8,128)(2,1)S(1)}, bf16[1,6,768,128]{3,2,1,0:T(8,128)(2,1)}, u32[]{:S(2)}) copy-start(bf16[1,6,768,128]{3,2,1,0:T(8,128)(2,1)} %param.5) | copy-start | bytes 3538948
  50.1 21.1 %all-to-all-start.1 = ((bf16[1,48,96,128]{3,1,0,2:T(8,128)(2,1)}), bf16[1,48,96,128]{3,1,0,2:T(8,128)(2,1)S(1)}, u32[]{:S(2)}, u32[]{:S(2)}) async-start(bf16[1,48,96,128]{3,1,0,2:T(8,128)(2,1)} %copy.226), calls=%async_computation.1 | async-start | bytes 2359296 | tf_op jit(solution)/shard_map/all_to_all | solution.py:61
  85.0 6.4 %copy-start.3 = (bf16[48,2,4,1024]{3,2,1,0:T(4,128)(2,1)S(1)}, bf16[48,2,4,1024]{3,2,1,0:T(4,128)(2,1)}, u32[]{:S(2)}) copy-start(bf16[48,2,4,1024]{3,2,1,0:T(4,128)(2,1)} %param.9) | copy-start | bytes 2359300
  85.0 30.9 %all-to-all-start.2 = ((bf16[1,384,12,128]{3,2,0,1:T(8,128)(2,1)}), bf16[1,384,12,128]{3,2,0,1:T(8,128)(2,1)}, u32[]{:S(2)}, u32[]{:S(2)}) async-start(bf16[1,384,12,128]{3,2,0,1:T(8,128)(2,1)} %copy.229), calls=%async_computation.2 | async-start | bytes 3145728 | tf_op jit(solution)/shard_map/all_to_all | solution.py:73
  204.4 21.6 %all-to-all-start.5 = ((bf16[1,48,96,128]{3,2,0,1:T(8,128)(2,1)}), bf16[1,48,96,128]{3,2,0,1:T(8,128)(2,1)}, u32[]{:S(2)}, u32[]{:S(2)}) async-start(bf16[1,48,96,128]{3,2,0,1:T(8,128)(2,1)} %copy.241), calls=%async_computation.5 | async-start | bytes 2359296 | tf_op jit(solution)/shard_map/all_to_all | solution.py:82
  291.1 23.0 %all-to-all-start.8 = ((bf16[1,384,12,128]{3,2,0,1:T(8,128)(2,1)}), bf16[1,384,12,128]{3,2,0,1:T(8,128)(2,1)S(1)}, u32[]{:S(2)}, u32[]{:S(2)}) async-start(bf16[1,384,12,128]{3,2,0,1:T(8,128)(2,1)} %copy.250), calls=%async_computation.8 | async-start | bytes 3145728 | tf_op jit(solution)/shard_map/all_to_all | solution.py:73
  375.2 31.8 %all-to-all-start.10 = ((bf16[1,384,12,128]{3,2,0,1:T(8,128)(2,1)}), bf16[1,384,12,128]{3,2,0,1:T(8,128)(2,1)S(1)}, u32[]{:S(2)}, u32[]{:S(2)}) async-start(bf16[1,384,12,128]{3,2,0,1:T(8,128)(2,1)} %copy.259), calls=%async_computation.10 | async-start | bytes 3145728 | tf_op jit(solution)/shard_map/all_to_all | solution.py:83
  380.3 97.0 %all-reduce.3.cloned.1.call-start = ((), (), s32[]{:S(2)}) async-start(), calls=%async_computation.12 | async-start | bytes 1572864 | tf_op jit(solution)/shard_map/psum | solution.py:109
  408.7 68.7 %copy-start.2 = (bf16[384,2,768]{2,1,0:T(2,128)(2,1)S(1)}, bf16[384,2,768]{2,1,0:T(2,128)(2,1)}, u32[]{:S(2)}) copy-start(bf16[384,2,768]{2,1,0:T(2,128)(2,1)} %copy.215) | copy-start | bytes 3538948
  408.7 133.3 %all-to-all-start.11 = ((bf16[1,48,96,128]{3,2,0,1:T(8,128)(2,1)}), bf16[1,48,96,128]{3,2,0,1:T(8,128)(2,1)S(1)}, u32[]{:S(2)}, u32[]{:S(2)}) async-start(bf16[1,48,96,128]{3,2,0,1:T(8,128)(2,1)} %copy.262), calls=%async_computation.11 | async-start | bytes 2359296 | tf_op jit(solution)/shard_map/all_to_all | solution.py:82
  412.4 126.7 %all-reduce.5.cloned.1.call-start = ((), (), s32[]{:S(2)}) async-start(), calls=%async_computation.13 | async-start | bytes 1572864 | tf_op jit(solution)/shard_map/psum | solution.py:109
  542.0 1.3 copy-start.4
  543.3 2.2 copy-start.1
Sparse Core Ops, SparseCore 0:
  407.0 70.2 all-reduce.2
  480.2 58.8 all-reduce.4
